TPU v7x, 128 devices: a whole 4x4x4 slice. The times are simulated.
128 devices in a mesh: space: 8 (over z_hi, x), blk: 16 (over y, z_lo, core).
Axes of the slice: x: 4, y: 4, z: 4 (z_hi: 2, z_lo: 2; z = z_hi * 2 + z_lo), core: 2. Of those that a mesh axis runs over, the one named last changes fastest.
Arguments:
- density: bfloat16 [12288, 128, 128], P(('space', 'blk')), may hold values from -6 to 6
- bra_table: bfloat16 [12288, 128, 256], P(('space', 'blk')), may hold values from -0.5 to 0.5
- ket_table: bfloat16 [12288, 128, 256], P(('space', 'blk')), may hold values from -0.5 to 0.5
- box_of_block: int32 [12288], P(('space', 'blk')), may hold values from 0 to 127
- leaf_src: int32 [1024, 27], P(('space', 'blk')), may hold values from 0 to 383
- leaf_type: int32 [1024, 27], P(('space', 'blk')), may hold values from 0 to 15
- coarse_src: int32 [128, 27], P(('space', 'blk')), may hold values from 0 to 127
- coarse_type: int32 [128, 27], P(('space', 'blk')), may hold values from 0 to 15
- translation: float32 [16, 256, 256], replicated, may hold values from -0.375 to 0.375
- upward_translation_table: float32 [8, 256, 256], replicated, may hold values from -0.375 to 0.375
Outputs:
- coulomb: bfloat16 [12288, 128, 128], P(('space', 'blk'))
- box_locals: float32 [1024, 256], P(('space', 'blk'))
All inputs are finite; a program needn't handle non-finite values.
Results may differ from a plain program's by a relative error of at most 0.0049.
Values sent between devices are 32-bit elements; how exact they have to be, the bound alone decides.
No kernel may reach another device: no remote copies, remote signals or barrier semaphores. Data moves between devices by JAX's collectives and lax.ppermute only.
A program may use at most 128 MiB of HBM per device.

v0:
```python
import jax
import jax.numpy as jnp
from jax import lax
from jax.sharding import PartitionSpec as P


def padded(block, sides, width):
    for axis, dim in sides:
        count = lax.axis_size(axis)
        forward = [(i, i + 1) for i in range(count - 1)]
        backward = [(target, source) for source, target in forward]
        low = lax.ppermute(
            lax.slice_in_dim(block, block.shape[dim] - width, None, axis=dim), axis, forward
        )
        high = lax.ppermute(lax.slice_in_dim(block, 0, width, axis=dim), axis, backward)
        block = jnp.concatenate([low, block, high], axis=dim)
    return block


def shards(
    density,
    bra_table,
    ket_table,
    box_of_block,
    leaf_src,
    leaf_type,
    coarse_src,
    coarse_type,
    translation,
    upward_translation_table,
):
    top_level_index = lax.Precision.HIGHEST
    n_blk = lax.axis_size("blk")
    box_dom = 8 * n_blk
    n_types = translation.shape[0]
    inner = jnp.einsum("bmn,bmk->bnk", density, bra_table, preferred_element_type=jnp.float32)
    moments = jnp.sum(inner * ket_table.astype(jnp.float32), axis=1)
    box_hot = (box_of_block[:, None] == jnp.arange(box_dom, dtype=jnp.int32)[None, :]).astype(
        jnp.float32
    )
    partial_moments = lax.dot_general(
        box_hot, moments, (((0,), (0,)), ((), ())), precision=top_level_index
    )
    held_boxes = lax.psum_scatter(partial_moments, "blk", scatter_dimension=0, tiled=True)
    domain = lax.all_gather(held_boxes, "blk", axis=0, tiled=True)
    window = padded(domain, (("space", 0),), box_dom)
    self_parent_index = jnp.einsum(
        "oe,ode->d", held_boxes, upward_translation_table, precision=top_level_index
    )[None, :]
    all_parents = lax.all_gather(self_parent_index, ("space", "blk"), axis=0, tiled=True)
    src_hot = (leaf_src[..., None] == jnp.arange(3 * box_dom, dtype=jnp.int32)).astype(jnp.float32)
    type_hot = (leaf_type[..., None] == jnp.arange(n_types, dtype=jnp.int32)).astype(jnp.float32)
    counts = jnp.einsum("blt,blj->btj", type_hot, src_hot, precision=top_level_index)
    gathered = jnp.einsum("btj,jk->btk", counts, window, precision=top_level_index)
    leaf_far = jnp.einsum("btk,tlk->bl", gathered, translation, precision=top_level_index)
    n_parents = all_parents.shape[0]
    csrc_hot = (coarse_src[..., None] == jnp.arange(n_parents, dtype=jnp.int32)).astype(jnp.float32)
    ctype_hot = (coarse_type[..., None] == jnp.arange(n_types, dtype=jnp.int32)).astype(jnp.float32)
    ccounts = jnp.einsum("pet,peq->ptq", ctype_hot, csrc_hot, precision=top_level_index)
    cgathered = jnp.einsum("ptq,qk->ptk", ccounts, all_parents, precision=top_level_index)
    parent_local_expansion = jnp.einsum(
        "ptk,tlk->pl", cgathered, translation, precision=top_level_index
    )
    downward_sent = jnp.einsum(
        "d,uds->us", parent_local_expansion[0], upward_translation_table, precision=top_level_index
    )
    box_locals = leaf_far + downward_sent
    domain_local = lax.all_gather(box_locals, "blk", axis=0, tiled=True)
    block_locals = jnp.dot(box_hot, domain_local, precision=top_level_index)
    scaled = (bra_table.astype(jnp.float32) * block_locals[:, None, :]).astype(jnp.bfloat16)
    coulomb = jnp.einsum(
        "bmk,bnk->bmn", scaled, ket_table, preferred_element_type=jnp.float32
    ).astype(jnp.bfloat16)
    return (coulomb, box_locals)


def solution(mesh):
    placed = (
        P(("space", "blk"), None, None),
        P(("space", "blk"), None, None),
        P(("space", "blk"), None, None),
        P(("space", "blk")),
        P(("space", "blk"), None),
        P(("space", "blk"), None),
        P(("space", "blk"), None),
        P(("space", "blk"), None),
        P(),
        P(),
    )
    return jax.shard_map(
        shards,
        mesh=mesh,
        in_specs=placed,
        out_specs=(P(("space", "blk"), None, None), P(("space", "blk"), None)),
        check_vma=False,
    )
```

profile of v0, /device:TPU:1, one launch (start us, length us, event | category | flops | bytes accessed | tf_op | source)
XLA Modules:
  0.0 324.4 jit_solution(17972422086320185214)
XLA Ops:
  7.2 0.0 copy-start
  7.2 0.0 copy-start.6
  7.2 0.0 copy-start.8
  7.2 0.0 copy-start.7
  7.2 0.0 copy-start.5
  7.2 0.0 copy-start.4
  7.2 0.0 reduce-scatter.2.cloned.1.call-start
  7.3 1.8 copy-done
  9.1 6.8 %multiply_reduce_fusion = f32[96,256]{1,0:T(8,128)S(1)} fusion(bf16[96,128,256]{2,1,0:T(8,128)(2,1)} %param.12, bf16[96,128,128]{2,1,0:T(8,128)(2,1)S(1)} %copy-done, bf16[96,128,256]{2,1,0:T(8,128)(2,1)} %param.11), kind=kOutput, calls=%fused_computation.1 | convolution fusion | flops 814718976 | bytes 15826944 | tf_op jit(solution)/shard_map/bmn,bmk->bnk/dot_general | solution.py:36
  15.9 0.0 copy-done.6
  15.9 1.0 fusion.15
  16.9 0.0 reduce-scatter.2.cloned.1.call-update
  16.9 0.0 copy-done.8
  16.9 0.0 copy-done.7
  16.9 0.2 fusion.21
  17.1 0.0 copy-done.5
  17.1 0.0 copy-done.4
  17.1 0.2 fusion.9
  17.4 60.2 %reduce-scatter.2.cloned.1.call-done = f32[8,256]{1,0:T(8,128)} async-done(((f32[128,256]{1,0:T(8,128)}), f32[8,256]{1,0:T(8,128)}) %reduce-scatter.2.cloned.1.call-update) | async-done | bytes 8208 | tf_op jit(solution)/shard_map/reduce_scatter | solution.py:44
  77.6 0.0 copy-start.2
  77.6 0.0 copy-start.1
  77.6 20.7 %all_gather.9 = f32[128,256]{1,0:T(8,128)S(1)} all-gather(f32[8,256]{1,0:T(8,128)} %reduce-scatter.2.cloned.1.call-done), channel_id=1, replica_groups=mesh['space'=8,'blk'=16] {'blk'}, dimensions={0}, use_global_device_ids=true | all-gather | bytes 139264 | tf_op jit(solution)/shard_map/all_gather | solution.py:45
  98.3 1.3 collective-permute-start.1
  99.6 4.0 %collective-permute-start = (f32[128,256]{1,0:T(8,128)S(1)}, f32[128,256]{1,0:T(8,128)S(1)}, u32[]{:S(2)}, u32[]{:S(2)}) collective-permute-start(f32[128,256]{1,0:T(8,128)S(1)} %all_gather.9), channel_id=1, source_target_pairs={{0,16},{16,32},{32,48},{48,64},{64,80},{80,96},{96,112},{1,17},{17... | collective-permute-start | bytes 393224 | tf_op jit(solution)/shard_map/ppermute | solution.py:12
  103.6 3.3 %convolution_bitcast_fusion.3 = f32[1,1,256]{2,1,0:T(1,128)S(1)} fusion(f32[8,256,256]{2,1,0:T(8,128)} %param.19, f32[8,256,1]{1,0,2:T(8,128)} %bitcast.43), kind=kOutput, calls=%fused_computation.9 | convolution fusion | flops 6291456 | bytes 2106368 | tf_op jit(solution)/shard_map/oe,ode->d/dot_general | solution.py:47
  107.0 175.0 %all-gather.1 = f32[128,1,256]{2,1,0:T(1,128)S(1)} all-gather(f32[1,1,256]{2,1,0:T(1,128)S(1)} %convolution_bitcast_fusion.3), channel_id=2, replica_groups=mesh['space'=8,'blk'=16] {'space','blk'}, dimensions={0}, use_global_device_ids=true | all-gather | bytes 132096 | tf_op jit(solution)/shard_map/all_gather | solution.py:50
  282.0 0.2 convolution_bitcast_fusion
  282.1 5.5 %convolution_bitcast_fusion.2 = f32[256,1,1]{0,1,2:T(1,128)S(1)} fusion(f32[16,256,256]{2,1,0:T(8,128)} %param.18, f32[16,256,1]{1,0,2:T(8,128)S(1)} %convolution_bitcast_fusion), kind=kOutput, calls=%fused_computation.8 | convolution fusion | flops 12582912 | bytes 4211712 | tf_op jit(solution)/shard_map/ptk,tlk->pl/dot_general | solution.py:61
  287.7 0.0 copy-done.2
  287.7 1.1 fusion.29
  288.8 0.0 collective-permute-done.1
  288.8 0.0 collective-permute-done
  288.8 0.4 fusion.4
  289.2 0.0 copy-done.1
  289.2 3.3 %fusion.3 = f32[8,256]{1,0:T(8,128)S(1)} fusion(f32[8,16,256]{2,0,1:T(8,128)S(1)} %fusion.4, f32[16,256,256]{2,1,0:T(8,128)S(1)} %copy-done.1, f32[1,8,256]{2,0,1:T(1,128)S(1)} %fusion.29), kind=kOutput, calls=%fused_computation.7 | convolution fusion | flops 100665344 | bytes 4341760 | tf_op jit(solution)/shard_map/btk,tlk->bl/dot_general | solution.py:55
  292.6 0.0 copy-start.3
  292.6 16.6 %all_gather.11 = f32[128,256]{1,0:T(8,128)S(1)} all-gather(f32[8,256]{1,0:T(8,128)S(1)} %fusion.3), channel_id=1, replica_groups=mesh['space'=8,'blk'=16] {'blk'}, dimensions={0}, use_global_device_ids=true | all-gather | bytes 139264 | tf_op jit(solution)/shard_map/all_gather | solution.py:68
  309.2 0.2 fusion.14
  309.4 8.1 %fusion.2 = bf16[96,128,128]{2,1,0:T(8,128)(2,1)} fusion(bf16[96,128,256]{2,1,0:T(8,128)(2,1)} %param.12, bf16[96,128,256]{2,1,0:T(8,128)(2,1)} %param.11, f32[96,256]{1,0:T(8,128)S(1)} %fusion.14), kind=kOutput, calls=%fused_computation.4 | convolution fusion | flops 816316416 | bytes 15826944 | tf_op jit(solution)/shard_map/bmk,bnk->bmn/dot_general | solution.py:71
  317.5 0.0 copy-done.3
Async XLA Ops:
  7.2 1.9 copy-start
  7.2 8.7 %copy-start.6 = (s32[96]{0:T(128)S(1)}, s32[96]{0:T(128)}, u32[]{:S(2)}) copy-start(s32[96]{0:T(128)} %param.13) | copy-start | bytes 1156
  7.2 9.7 %copy-start.8 = (s32[1,27]{1,0:T(1,128)S(1)}, s32[1,27]{1,0:T(1,128)}, u32[]{:S(2)}) copy-start(s32[1,27]{1,0:T(1,128)} %param.17) | copy-start | bytes 328
  7.2 9.7 %copy-start.7 = (s32[1,27]{1,0:T(1,128)S(1)}, s32[1,27]{1,0:T(1,128)}, u32[]{:S(2)}) copy-start(s32[1,27]{1,0:T(1,128)} %param.16) | copy-start | bytes 328
  7.2 9.9 %copy-start.5 = (s32[8,27]{1,0:T(8,128)S(1)}, s32[8,27]{1,0:T(8,128)}, u32[]{:S(2)}) copy-start(s32[8,27]{1,0:T(8,128)} %param.15) | copy-start | bytes 2596
  7.2 9.9 %copy-start.4 = (s32[8,27]{1,0:T(8,128)S(1)}, s32[8,27]{1,0:T(8,128)}, u32[]{:S(2)}) copy-start(s32[8,27]{1,0:T(8,128)} %param.14) | copy-start | bytes 2596
  7.2 70.4 %reduce-scatter.2.cloned.1.call-start = ((), (), s32[]{:S(2)}) async-start(), calls=%async_computation.1 | async-start | bytes 139264 | tf_op jit(solution)/shard_map/reduce_scatter | solution.py:44
  77.6 210.1 %copy-start.2 = (f32[8,256,256]{2,1,0:T(8,128)S(1)}, f32[8,256,256]{2,1,0:T(8,128)}, u32[]{:S(2)}) copy-start(f32[8,256,256]{2,1,0:T(8,128)} %param.19) | copy-start | bytes 6291460
  77.6 211.6 %copy-start.1 = (f32[16,256,256]{2,1,0:T(8,128)S(1)}, f32[16,256,256]{2,1,0:T(8,128)}, u32[]{:S(2)}) copy-start(f32[16,256,256]{2,1,0:T(8,128)} %param.18) | copy-start | bytes 12582916
  98.3 190.5 %collective-permute-start.1 = (f32[128,256]{1,0:T(8,128)S(1)}, f32[128,256]{1,0:T(8,128)S(1)}, u32[]{:S(2)}, u32[]{:S(2)}) collective-permute-start(f32[128,256]{1,0:T(8,128)S(1)} %all_gather.9), channel_id=1, source_target_pairs={{16,0},{32,16},{48,32},{64,48},{80,64},{96,80},{112,96},{17,1},{33... | collective-permute-start | bytes 393224 | tf_op jit(solution)/shard_map/ppermute | solution.py:15
  99.6 189.2 %collective-permute-start = (f32[128,256]{1,0:T(8,128)S(1)}, f32[128,256]{1,0:T(8,128)S(1)}, u32[]{:S(2)}, u32[]{:S(2)}) collective-permute-start(f32[128,256]{1,0:T(8,128)S(1)} %all_gather.9), channel_id=1, source_target_pairs={{0,16},{16,32},{32,48},{48,64},{64,80},{80,96},{96,112},{1,17},{17... | collective-permute-start | bytes 393224 | tf_op jit(solution)/shard_map/ppermute | solution.py:12
  292.6 24.9 %copy-start.3 = (f32[8,256]{1,0:T(8,128)}, f32[8,256]{1,0:T(8,128)S(1)}, u32[]{:S(2)}) copy-start(f32[8,256]{1,0:T(8,128)S(1)} %fusion.3) | copy-start | bytes 24580
Sparse Core Ops, SparseCore 0:
  17.0 60.5 reduce-scatter.1
where the time goes:
time: 325 us; the launch traced here: 324 us
  blocking collectives  212 us (65%)
  waiting for transfers between devices  60.3 us (19%)
  matrix products  30.5 us (9%)
  between operations  14.2 us (4%)
  starting transfers between devices  5.31 us (2%)
    all_gather x1, blocking collectives, shards(): lax.all_gather(self_parent_index, ('space', 'blk'), axis=0, tiled=True)  175 us
    reduce_scatter x1, waiting for transfers between devices, shards(): lax.psum_scatter(partial_moments, 'blk', scatter_dimension=0, tiled=True)  60.2 us
    all_gather x1, blocking collectives, shards(): domain = lax.all_gather(held_boxes, 'blk', axis=0, tiled=True)  20.7 us
    all_gather x1, blocking collectives, shards(): domain_local = lax.all_gather(box_locals, 'blk', axis=0, tiled=True)  16.6 us
    dot_general x1, matrix products, shards(): jnp.einsum('bmk,bnk->bmn', scaled, ket_table, preferred_element_type=jnp....  8.08 us
    dot_general x1, matrix products, shards(): jnp.einsum('bmn,bmk->bnk', density, bra_table, preferred_element_type=jnp...  6.82 us
  transfers between devices with their start and end apart: 3, of which 1 were waited for; matrix products, arithmetic and copies ran while one was open for 3% of the time, Pallas kernels for 0%

commit v1 on v0

--- a/solution.py
+++ b/solution.py
@@ -47,7 +47,16 @@
     self_parent_index = jnp.einsum(
         "oe,ode->d", held_boxes, upward_translation_table, precision=top_level_index
     )[None, :]
-    all_parents = lax.all_gather(self_parent_index, ("space", "blk"), axis=0, tiled=True)
+    knots_lift = lambda base_x: jnp.concatenate(
+        lax.all_to_all(
+            jnp.stack([base_x for _ in range(lax.axis_size(("space", "blk")))]),
+            axis_name=("space", "blk"),
+            split_axis=0,
+            concat_axis=0,
+        ),
+        axis=0,
+    )
+    all_parents = knots_lift(self_parent_index)
     src_hot = (leaf_src[..., None] == jnp.arange(3 * box_dom, dtype=jnp.int32)).astype(jnp.float32)
     type_hot = (leaf_type[..., None] == jnp.arange(n_types, dtype=jnp.int32)).astype(jnp.float32)
     counts = jnp.einsum("blt,blj->btj", type_hot, src_hot, precision=top_level_index)

time: 325 us -> 169 us (0.52)
  blocking collectives: 212 us -> 39 us
  starting transfers between devices: 5.31 us -> 16.5 us
    all_gather x1 -> x0, blocking collectives: 175 us -> none  [shards(): lax.all_gather(self_parent_index, ('space', 'blk'), axis=0, tiled=True)]
    all_to_all x0 -> x1, starting transfers between devices: none -> 10.5 us  [shards(): lax.all_to_all(jnp.stack([base_x for _ in range(lax.axis_size(('space', '...]
  transfers between devices with their start and end apart: 3 -> 4, of which waited for: 1 -> 1; matrix products, arithmetic and copies ran while one was open for 3% -> 5% of each run, Pallas kernels for 0% -> 0%
where the time goes in v1:
time: 169 us; the launch traced here: 166 us
  waiting for transfers between devices  60.4 us (36%)
  blocking collectives  39 us (23%)
  matrix products  33.3 us (20%)
  starting transfers between devices  16.5 us (10%)
  between operations  14.2 us (8%)
  local copies, waits for them, and re-layouts  2.56 us (2%)
    reduce_scatter x1, waiting for transfers between devices, shards(): lax.psum_scatter(partial_moments, 'blk', scatter_dimension=0, tiled=True)  60.4 us
    all_gather x1, blocking collectives, shards(): domain = lax.all_gather(held_boxes, 'blk', axis=0, tiled=True)  22.2 us
    all_gather x1, blocking collectives, shards(): domain_local = lax.all_gather(box_locals, 'blk', axis=0, tiled=True)  16.9 us
    all_to_all x1, starting transfers between devices, shards(): lax.all_to_all(jnp.stack([base_x for _ in range(lax.axis_size(('space', '...  10.5 us
    dot_general x1, matrix products, shards(): jnp.einsum('bmk,bnk->bmn', scaled, ket_table, preferred_element_type=jnp....  8.08 us
    dot_general x1, matrix products, shards(): jnp.einsum('bmn,bmk->bnk', density, bra_table, preferred_element_type=jnp...  6.82 us
    dot_general x1, matrix products, shards(): jnp.einsum('ptk,tlk->pl', cgathered, translation, precision=top_level_index)  5.7 us
    ppermute x1, starting transfers between devices, padded(): lax.ppermute(lax.slice_in_dim(block, block.shape[dim] - width, None, axis...  4.64 us
  transfers between devices with their start and end apart: 4, of which 1 were waited for; matrix products, arithmetic and copies ran while one was open for 5% of the time, Pallas kernels for 0%

profile of v1, /device:TPU:1, one launch (start us, length us, event | category | flops | bytes accessed | tf_op | source)
XLA Modules:
  0.0 166.0 jit_solution(4582340891237530754)
XLA Ops:
  7.2 0.0 copy-start
  7.2 0.0 copy-start.5
  7.2 0.0 copy-start.4
  7.2 0.0 copy-start.3
  7.2 0.0 copy-start.7
  7.2 0.0 copy-start.6
  7.2 0.0 reduce-scatter.2.cloned.1.call-start
  7.3 1.8 %copy-done = bf16[96,128,128]{2,1,0:T(8,128)(2,1)S(1)} copy-done((bf16[96,128,128]{2,1,0:T(8,128)(2,1)S(1)}, bf16[96,128,128]{2,1,0:T(8,128)(2,1)}, u32[]{:S(2)}) %copy-start) | copy-done | bytes 3145752
  9.1 6.8 %multiply_reduce_fusion = f32[96,256]{1,0:T(8,128)S(1)} fusion(bf16[96,128,256]{2,1,0:T(8,128)(2,1)} %param.12, bf16[96,128,128]{2,1,0:T(8,128)(2,1)S(1)} %copy-done, bf16[96,128,256]{2,1,0:T(8,128)(2,1)} %param.11), kind=kOutput, calls=%fused_computation.1 | convolution fusion | flops 814718976 | bytes 15826944 | tf_op jit(solution)/shard_map/bmn,bmk->bnk/dot_general | solution.py:36
  15.9 0.0 copy-done.5
  15.9 1.0 fusion.16
  16.9 0.0 reduce-scatter.2.cloned.1.call-update
  16.9 0.0 copy-done.4
  16.9 0.0 copy-done.3
  16.9 0.3 fusion.9
  17.3 60.4 %reduce-scatter.2.cloned.1.call-done = f32[8,256]{1,0:T(8,128)} async-done(((f32[128,256]{1,0:T(8,128)}), f32[8,256]{1,0:T(8,128)}) %reduce-scatter.2.cloned.1.call-update) | async-done | bytes 8208 | tf_op jit(solution)/shard_map/reduce_scatter | solution.py:44
  77.6 3.3 %fusion.23 = f32[1,256,1]{1,0,2:T(1,128)S(1)} fusion(f32[8,256,256]{2,1,0:T(8,128)} %param.19, f32[8,256,1]{1,0,2:T(8,128)} %bitcast.40), kind=kOutput, calls=%fused_computation.32 | convolution fusion | flops 6291456 | bytes 2106368 | tf_op jit(solution)/shard_map/oe,ode->d/dot_general | solution.py:47
  80.9 0.7 stack.3
  81.7 10.5 %all-to-all-start = ((f32[128,1,256]{2,1,0:T(1,128)}), f32[128,1,256]{2,1,0:T(1,128)S(1)}, u32[]{:S(2)}, u32[]{:S(2)}) async-start(f32[128,1,256]{2,1,0:T(1,128)} %stack.3), calls=%async_computation.1 | async-start | bytes 262144 | tf_op jit(solution)/shard_map/all_to_all | solution.py:51
  92.2 0.0 copy-done.7
  92.2 0.0 copy-done.6
  92.3 0.2 fusion.21
  92.4 22.2 %all_gather.6 = f32[128,256]{1,0:T(8,128)} all-gather(f32[8,256]{1,0:T(8,128)} %reduce-scatter.2.cloned.1.call-done), channel_id=1, replica_groups=mesh['space'=8,'blk'=16] {'blk'}, dimensions={0}, use_global_device_ids=true | all-gather | bytes 139264 | tf_op jit(solution)/shard_map/all_gather | solution.py:45
  114.6 1.3 collective-permute-start.1
  115.9 4.6 %collective-permute-start = (f32[128,256]{1,0:T(8,128)}, f32[128,256]{1,0:T(8,128)}, u32[]{:S(2)}, u32[]{:S(2)}) collective-permute-start(f32[128,256]{1,0:T(8,128)} %all_gather.6), channel_id=1, source_target_pairs={{0,16},{16,32},{32,48},{48,64},{64,80},{80,96},{96,112},{1,17},{17... | collective-permute-start | bytes 393224 | tf_op jit(solution)/shard_map/ppermute | solution.py:12
  120.5 0.0 all-to-all-done
  120.6 0.0 copy-start.1
  120.6 0.2 convolution_bitcast_fusion
  120.7 5.7 %convolution_bitcast_fusion.2 = f32[256,1,1]{0,1,2:T(1,128)S(1)} fusion(f32[16,256,256]{2,1,0:T(8,128)} %param.18, f32[16,256,1]{1,0,2:T(8,128)S(1)} %convolution_bitcast_fusion), kind=kOutput, calls=%fused_computation.8 | convolution fusion | flops 12582912 | bytes 4211712 | tf_op jit(solution)/shard_map/ptk,tlk->pl/dot_general | solution.py:70
  126.4 2.7 %fusion.30 = f32[1,8,256]{2,0,1:T(1,128)S(1)} fusion(f32[256,1,1]{0,1,2:T(1,128)S(1)} %convolution_bitcast_fusion.2, f32[8,256,256]{2,1,0:T(8,128)} %param.19), kind=kOutput, calls=%fused_computation.39 | convolution fusion | flops 6291456 | bytes 2106368 | tf_op jit(solution)/shard_map/d,uds->us/dot_general | solution.py:73
  129.1 0.0 collective-permute-done.1
  129.1 0.0 collective-permute-done
  129.1 1.4 fusion.4
  130.6 0.0 copy-done.1
  130.6 3.3 %fusion.3 = f32[8,256]{1,0:T(8,128)S(1)} fusion(f32[8,16,256]{2,0,1:T(8,128)S(1)} %fusion.4, f32[16,256,256]{2,1,0:T(8,128)S(1)} %copy-done.1, f32[1,8,256]{2,0,1:T(1,128)S(1)} %fusion.30), kind=kOutput, calls=%fused_computation.7 | convolution fusion | flops 100665344 | bytes 4341760 | tf_op jit(solution)/shard_map/btk,tlk->bl/dot_general | solution.py:64
  133.9 0.0 copy-start.2
  133.9 16.9 %all_gather.7 = f32[128,256]{1,0:T(8,128)S(1)} all-gather(f32[8,256]{1,0:T(8,128)S(1)} %fusion.3), channel_id=1, replica_groups=mesh['space'=8,'blk'=16] {'blk'}, dimensions={0}, use_global_device_ids=true | all-gather | bytes 139264 | tf_op jit(solution)/shard_map/all_gather | solution.py:77
  150.8 0.2 fusion.15
  151.0 8.1 %fusion.2 = bf16[96,128,128]{2,1,0:T(8,128)(2,1)} fusion(bf16[96,128,256]{2,1,0:T(8,128)(2,1)} %param.12, bf16[96,128,256]{2,1,0:T(8,128)(2,1)} %param.11, f32[96,256]{1,0:T(8,128)S(1)} %fusion.15), kind=kOutput, calls=%fused_computation.4 | convolution fusion | flops 816316416 | bytes 15826944 | tf_op jit(solution)/shard_map/bmk,bnk->bmn/dot_general | solution.py:80
  159.1 0.0 copy-done.2
Async XLA Ops:
  7.2 1.9 %copy-start = (bf16[96,128,128]{2,1,0:T(8,128)(2,1)S(1)}, bf16[96,128,128]{2,1,0:T(8,128)(2,1)}, u32[]{:S(2)}) copy-start(bf16[96,128,128]{2,1,0:T(8,128)(2,1)} %param.10) | copy-start | bytes 9437188
  7.2 8.7 %copy-start.5 = (s32[96]{0:T(128)S(1)}, s32[96]{0:T(128)}, u32[]{:S(2)}) copy-start(s32[96]{0:T(128)} %param.13) | copy-start | bytes 1156
  7.2 9.7 %copy-start.4 = (s32[8,27]{1,0:T(8,128)S(1)}, s32[8,27]{1,0:T(8,128)}, u32[]{:S(2)}) copy-start(s32[8,27]{1,0:T(8,128)} %param.15) | copy-start | bytes 2596
  7.2 9.7 %copy-start.3 = (s32[8,27]{1,0:T(8,128)S(1)}, s32[8,27]{1,0:T(8,128)}, u32[]{:S(2)}) copy-start(s32[8,27]{1,0:T(8,128)} %param.14) | copy-start | bytes 2596
  7.2 85.0 %copy-start.7 = (s32[1,27]{1,0:T(1,128)S(1)}, s32[1,27]{1,0:T(1,128)}, u32[]{:S(2)}) copy-start(s32[1,27]{1,0:T(1,128)} %param.17) | copy-start | bytes 328
  7.2 85.0 %copy-start.6 = (s32[1,27]{1,0:T(1,128)S(1)}, s32[1,27]{1,0:T(1,128)}, u32[]{:S(2)}) copy-start(s32[1,27]{1,0:T(1,128)} %param.16) | copy-start | bytes 328
  7.2 70.4 %reduce-scatter.2.cloned.1.call-start = ((), (), s32[]{:S(2)}) async-start(), calls=%async_computation.2 | async-start | bytes 139264 | tf_op jit(solution)/shard_map/reduce_scatter | solution.py:44
  81.7 38.9 %all-to-all-start = ((f32[128,1,256]{2,1,0:T(1,128)}), f32[128,1,256]{2,1,0:T(1,128)S(1)}, u32[]{:S(2)}, u32[]{:S(2)}) async-start(f32[128,1,256]{2,1,0:T(1,128)} %stack.3), calls=%async_computation.1 | async-start | bytes 262144 | tf_op jit(solution)/shard_map/all_to_all | solution.py:51
  114.6 14.5 %collective-permute-start.1 = (f32[128,256]{1,0:T(8,128)}, f32[128,256]{1,0:T(8,128)}, u32[]{:S(2)}, u32[]{:S(2)}) collective-permute-start(f32[128,256]{1,0:T(8,128)} %all_gather.6), channel_id=1, source_target_pairs={{16,0},{32,16},{48,32},{64,48},{80,64},{96,80},{112,96},{17,1},{33... | collective-permute-start | bytes 393224 | tf_op jit(solution)/shard_map/ppermute | solution.py:15
  115.9 13.2 %collective-permute-start = (f32[128,256]{1,0:T(8,128)}, f32[128,256]{1,0:T(8,128)}, u32[]{:S(2)}, u32[]{:S(2)}) collective-permute-start(f32[128,256]{1,0:T(8,128)} %all_gather.6), channel_id=1, source_target_pairs={{0,16},{16,32},{32,48},{48,64},{64,80},{80,96},{96,112},{1,17},{17... | collective-permute-start | bytes 393224 | tf_op jit(solution)/shard_map/ppermute | solution.py:12
  120.6 10.0 %copy-start.1 = (f32[16,256,256]{2,1,0:T(8,128)S(1)}, f32[16,256,256]{2,1,0:T(8,128)}, u32[]{:S(2)}) copy-start(f32[16,256,256]{2,1,0:T(8,128)} %param.18) | copy-start | bytes 12582916
  133.9 25.2 %copy-start.2 = (f32[8,256]{1,0:T(8,128)}, f32[8,256]{1,0:T(8,128)S(1)}, u32[]{:S(2)}) copy-start(f32[8,256]{1,0:T(8,128)S(1)} %fusion.3) | copy-start | bytes 24580
Sparse Core Ops, SparseCore 0:
  17.0 60.5 reduce-scatter.1
